TPU v7x, 512 devices: a whole 4x8x8 slice. The times are simulated.
512 devices in a mesh: segment: 16 (over z, core), mp: 32 (over y, x).
Axes of the slice: x: 4, y: 8, z: 8, core: 2. Of those that a mesh axis runs over, the one named last changes fastest.
Arguments:
- rows: bfloat16 [16, 2, 128, 8192], P('segment', None, None, 'mp'), may hold values from -6 to 6
- carry: bfloat16 [16, 128, 8192], P('segment', None, 'mp'), may hold values from -6 to 6
- weights: bfloat16 [16, 2, 8192, 4096], P('segment', None, None, 'mp'), may hold values from -1.1932427 to 1.1932427
- neighbours: int32 [16, 2, 2, 2], P('segment'), may hold values from 0 to 7, all different within a row
Outputs:
- passed: bfloat16 [16, 128, 8192], P('segment', None, 'mp')
- returned: bfloat16 [16, 128, 8192], P('segment', None, 'mp')
- kv_grad: bfloat16 [1024, 2, 4096], P(None, None, 'mp')
Inputs may be any that keep to these rules, and one draw needn't show every extreme that they name: Each group's 2 neighbours are different pool blocks; pool blocks are numbered by encoder segment in order, then by row.
All inputs are finite; a program needn't handle non-finite values.
Results may differ from a plain program's by a relative error of at most 0.02.
The roundings to bfloat16 on the way count: a program that leaves them out, or rounds other values in their place, can miss the bound.
Values may be sent and summed in bfloat16 or wider, within the bound.
No kernel may reach another device: no remote copies, remote signals or barrier semaphores. Data moves between devices by JAX's collectives and lax.ppermute only.
A program may use at most 64 MiB of HBM per device.

v0:
```python
import math
import jax
import jax.numpy as jnp
from jax import lax
from jax.sharding import PartitionSpec as P

GROUP = 64
NBLEN = 128
NEIGH = 2


def from_behind(x, axis, by):
    devices = lax.axis_size(axis)
    return lax.ppermute(x, axis, [(i, (i + by) % devices) for i in range(devices)])


def attend(queries, key_rows, score_scale):
    scores = (
        jnp.einsum("cqd,ckd->cqk", queries, key_rows, preferred_element_type=jnp.float32)
        * score_scale
    )
    soft = jax.nn.softmax(scores, axis=-1)
    return (soft, soft.astype(jnp.bfloat16))


def attend_back(queries, key_rows, value_rows, soft, rounded, upstream, score_scale):
    d_soft = jnp.einsum("cqd,ckd->cqk", upstream, value_rows, preferred_element_type=jnp.float32)
    grad_values = jnp.einsum("cqk,cqd->ckd", rounded, upstream, preferred_element_type=jnp.float32)
    d_scores = soft * (d_soft - jnp.sum(d_soft * soft, axis=-1, keepdims=True))
    grad_queries = (
        jnp.einsum("cqk,ckd->cqd", d_scores, key_rows.astype(jnp.float32)) * score_scale
    ).astype(jnp.bfloat16)
    grad_keys = jnp.einsum("cqk,cqd->ckd", d_scores, queries.astype(jnp.float32)) * score_scale
    return (grad_queries, grad_keys, grad_values)


def head_sum(term, axis):
    devices = lax.axis_size(axis)
    parts = term.astype(jnp.bfloat16).reshape(devices, term.shape[0] // devices, term.shape[1])
    moved = lax.all_to_all(parts, axis, 0, 0, tiled=True)
    return jnp.sum(moved.astype(jnp.float32), axis=0).T


def segment_sum(contrib, axis):
    devices = lax.axis_size(axis)
    parts = contrib.reshape(devices, contrib.shape[0] // devices, contrib.shape[1])
    moved = lax.all_to_all(parts, axis, 0, 0, tiled=True)
    summed = jnp.sum(moved.astype(jnp.float32), axis=0).astype(jnp.bfloat16)
    spread = jnp.broadcast_to(summed[None], (devices,) + summed.shape)
    return lax.all_to_all(spread, axis, 0, 0, tiled=True).reshape(contrib.shape)


def per_device(rows, carry, weights, neighbours):
    segments = lax.axis_size("segment")
    encoders = segments // 4
    first_encoder = segments - encoders
    is_encoder = lax.axis_index("segment") >= first_encoder
    local_rows = rows[0]
    local_carry = carry[0]
    full_rows, full_carry = (
        lax.all_gather(local_rows, "mp", axis=2, tiled=True),
        lax.all_gather(local_carry, "mp", axis=1, tiled=True),
    )
    tokens = local_rows.shape[1]
    width = full_rows.shape[2]
    head = weights.shape[3]
    w_query = weights[0, 0]
    w_out = weights[0, 1]

    def encode():
        flat = full_rows.reshape(2 * tokens, width)
        keyval = jnp.concatenate(
            [
                jnp.dot(flat, w_query, preferred_element_type=jnp.float32),
                jnp.dot(flat, w_out, preferred_element_type=jnp.float32),
            ],
            axis=-1,
        ).astype(jnp.bfloat16)
        return (keyval, jnp.zeros((2 * tokens, head), jnp.bfloat16))

    def decode():
        queries = jnp.dot(
            full_rows.reshape(2 * tokens, width), w_query, preferred_element_type=jnp.float32
        ).astype(jnp.bfloat16)
        return (jnp.zeros((2 * tokens, 2 * head), jnp.bfloat16), queries)

    encoded, queries = lax.cond(is_encoder, encode, decode)
    per_encoder = 2 * tokens // NBLEN
    pool_blocks = encoders * per_encoder
    collected = lax.all_gather(encoded, "segment", axis=0, tiled=True)
    pool = collected[first_encoder * 2 * tokens :].reshape(pool_blocks, NBLEN, 2 * head)
    groups = tokens // GROUP
    local_nbr = neighbours[0]
    score_scale = 1.0 / math.sqrt(head)
    query_blocks = queries.reshape(2, groups, GROUP, head)

    def fetch(batch):
        picked = pool[local_nbr[batch]].reshape(groups, NEIGH * NBLEN, 2 * head)
        return (picked[..., :head], picked[..., head:])

    keys_fwd, values_fwd = fetch(0)
    soft_fwd, rounded_fwd = attend(query_blocks[0], keys_fwd, score_scale)
    mixed = jnp.einsum(
        "cqk,ckd->cqd", rounded_fwd, values_fwd, preferred_element_type=jnp.float32
    ).astype(jnp.bfloat16)
    mixed_flat = mixed.reshape(tokens, head)
    piece = w_out
    out_sum = head_sum(
        lax.dot_general(
            piece, mixed_flat, (((1,), (1,)), ((), ())), preferred_element_type=jnp.float32
        ),
        "mp",
    )
    forward_rows = (local_rows[0].astype(jnp.float32) + out_sum).astype(jnp.bfloat16)
    forward_rows = jnp.where(is_encoder, local_carry, forward_rows)
    passed = from_behind(forward_rows[None], "segment", 1)
    upstream = (
        jnp.dot(full_carry, w_out, preferred_element_type=jnp.float32)
        .astype(jnp.bfloat16)
        .reshape(groups, GROUP, head)
    )
    keys_back, values_back = fetch(1)
    soft_back, rounded_back = attend(query_blocks[1], keys_back, score_scale)
    grad_queries, grad_keys, grad_values = attend_back(
        query_blocks[1], keys_back, values_back, soft_back, rounded_back, upstream, score_scale
    )
    grad_flat = grad_queries.reshape(tokens, head)
    piece = w_query
    grad_input = head_sum(
        lax.dot_general(
            piece, grad_flat, (((1,), (1,)), ((), ())), preferred_element_type=jnp.float32
        ),
        "mp",
    )
    back = local_carry.astype(jnp.float32) + grad_input
    back_rows = jnp.where(is_encoder, local_carry, back.astype(jnp.bfloat16))
    returned = from_behind(back_rows[None], "segment", -1)
    onehot = (
        local_nbr[1][..., None] == jnp.arange(pool_blocks, dtype=jnp.int32)[None, None, :]
    ).astype(jnp.float32)
    grad_keyval = jnp.concatenate([grad_keys, grad_values], axis=-1).reshape(
        groups, NEIGH, NBLEN, 2 * head
    )
    contrib = jnp.einsum("cbp,cbrf->prf", onehot, grad_keyval)
    contrib = jnp.where(is_encoder, jnp.zeros_like(contrib), contrib)
    pooled = segment_sum(
        contrib.astype(jnp.bfloat16).reshape(pool_blocks * NBLEN, 2 * head), "segment"
    )
    kv_grad = pooled.reshape(pool_blocks * NBLEN, 2, head)
    return (passed, returned, kv_grad)


def solution(mesh):
    placed = (
        P("segment", None, None, "mp"),
        P("segment", None, "mp"),
        P("segment", None, None, "mp"),
        P("segment", None, None, None),
    )
    return jax.shard_map(
        per_device,
        mesh=mesh,
        in_specs=placed,
        out_specs=(P("segment", None, "mp"), P("segment", None, "mp"), P(None, None, "mp")),
        check_vma=False,
    )
```

profile of v0, /device:TPU:1, one launch (start us, length us, event | category | flops | bytes accessed | tf_op | source)
XLA Modules:
  0.0 407.9 jit_solution(1906226420023038693)
XLA Ops:
  8.7 3.8 slice_bitcast_fusion
  12.5 89.2 %all-gather.8.cloned.1.call-done = bf16[1,2,128,8192]{3,2,1,0:T(8,128)(2,1)} async-done(((bf16[1,2,128,256]{3,2,1,0:T(8,128)(2,1)}), bf16[1,2,128,8192]{3,2,1,0:T(8,128)(2,1)}) %all-gather.8.cloned.1.call-update) | async-done | bytes 4194320 | tf_op jit(solution)/shard_map/all_gather | solution.py:61
  101.8 3.5 conditional.1
  101.8 3.4 convolution_convert_fusion
  106.2 79.5 %all-gather.10.cloned.1.call-done = bf16[1,128,8192]{2,1,0:T(8,128)(2,1)} async-done(((bf16[1,128,256]{2,1,0:T(8,128)(2,1)}), bf16[1,128,8192]{2,1,0:T(8,128)(2,1)}) %all-gather.10.cloned.1.call-update) | async-done | bytes 2097168 | tf_op jit(solution)/shard_map/all_gather | solution.py:62
  185.7 2.9 fusion.11
  188.6 45.9 %all-gather.6.cloned.1.call-done = bf16[4096,256]{1,0:T(8,128)(2,1)} async-done(((bf16[256,256]{1,0:T(8,128)(2,1)}), bf16[4096,256]{1,0:T(8,128)(2,1)}) %all-gather.6.cloned.1.call-update) | async-done | bytes 2097168 | tf_op jit(solution)/shard_map/all_gather | solution.py:90
  234.5 1.1 slice.67
  238.8 0.9 copy.19
  239.7 4.4 %all-to-all-start.2 = ((bf16[16,64,256]{2,1,0:T(8,128)(2,1)}), bf16[16,64,256]{2,1,0:T(8,128)(2,1)S(1)}, u32[]{:S(2)}, u32[]{:S(2)}) async-start(bf16[16,64,256]{2,1,0:T(8,128)(2,1)} %bitcast.28), calls=%async_computation.2 | async-start | bytes 1048576 | tf_op jit(solution)/shard_map/all_to_all | solution.py:47
  244.5 2.3 convolution_convert_fusion.3
  246.8 1.6 copy.25
  248.4 13.1 %all-to-all-done.2 = bf16[16,64,256]{2,1,0:T(8,128)(2,1)S(1)} async-done(((bf16[16,64,256]{2,1,0:T(8,128)(2,1)}), bf16[16,64,256]{2,1,0:T(8,128)(2,1)S(1)}, u32[]{:S(2)}, u32[]{:S(2)}) %all-to-all-start.2) | async-done | bytes 524320 | tf_op jit(solution)/shard_map/all_to_all | solution.py:47
  261.5 9.3 %all-to-all-start.1 = ((bf16[32,256,128]{1,2,0:T(8,128)(2,1)}), bf16[32,256,128]{1,2,0:T(8,128)(2,1)S(1)}, u32[]{:S(2)}, u32[]{:S(2)}) async-start(bf16[32,256,128]{1,2,0:T(8,128)(2,1)} %bitcast.105), calls=%async_computation.1 | async-start | bytes 4194304 | tf_op jit(solution)/shard_map/all_to_all | solution.py:40
  272.1 2.3 convolution_convert_fusion.4
  274.4 1.6 copy.26
  276.0 45.4 %all-to-all-done.1 = bf16[32,256,128]{1,2,0:T(8,128)(2,1)S(1)} async-done(((bf16[32,256,128]{1,2,0:T(8,128)(2,1)}), bf16[32,256,128]{1,2,0:T(8,128)(2,1)S(1)}, u32[]{:S(2)}, u32[]{:S(2)}) %all-to-all-start.1) | async-done | bytes 2097184 | tf_op jit(solution)/shard_map/all_to_all | solution.py:40
  321.4 5.1 %all-to-all-start = ((bf16[32,256,128]{1,2,0:T(8,128)(2,1)}), bf16[32,256,128]{1,2,0:T(8,128)(2,1)}, u32[]{:S(2)}, u32[]{:S(2)}) async-start(bf16[32,256,128]{1,2,0:T(8,128)(2,1)} %bitcast.106), calls=%async_computation | async-start | bytes 4194304 | tf_op jit(solution)/shard_map/all_to_all | solution.py:40
  326.7 48.3 %all-to-all-done = bf16[32,256,128]{1,2,0:T(8,128)(2,1)} async-done(((bf16[32,256,128]{1,2,0:T(8,128)(2,1)}), bf16[32,256,128]{1,2,0:T(8,128)(2,1)}, u32[]{:S(2)}, u32[]{:S(2)}) %all-to-all-start) | async-done | bytes 2097184 | tf_op jit(solution)/shard_map/all_to_all | solution.py:40
  375.9 6.0 %all-to-all-start.3 = ((bf16[16,64,256]{2,1,0:T(8,128)(2,1)}), bf16[16,64,256]{2,1,0:T(8,128)(2,1)S(1)}, u32[]{:S(2)}, u32[]{:S(2)}) async-start(bf16[16,64,256]{2,1,0:T(8,128)(2,1)} %broadcast_in_dim.11), calls=%async_computation.3 | async-start | bytes 1048576 | tf_op jit(solution)/shard_map/all_to_all | solution.py:50
  382.2 1.9 convert_reduce_fusion.1
  384.1 1.7 collective-permute-start
  385.8 13.4 %all-to-all-done.3 = bf16[16,64,256]{2,1,0:T(8,128)(2,1)S(1)} async-done(((bf16[16,64,256]{2,1,0:T(8,128)(2,1)}), bf16[16,64,256]{2,1,0:T(8,128)(2,1)S(1)}, u32[]{:S(2)}, u32[]{:S(2)}) %all-to-all-start.3) | async-done | bytes 524320 | tf_op jit(solution)/shard_map/all_to_all | solution.py:50
  399.2 0.9 reshape_reshape.7
  (47 shorter events, 9.7 us)
Async XLA Ops:
  7.2 94.6 %all-gather.8.cloned.1.call-start = ((), (), s32[]{:S(2)}) async-start(), calls=%async_computation.5 | async-start | bytes 4325376 | tf_op jit(solution)/shard_map/all_gather | solution.py:61
  7.9 177.8 %all-gather.10.cloned.1.call-start = ((), (), s32[]{:S(2)}) async-start(), calls=%async_computation.6 | async-start | bytes 2162688 | tf_op jit(solution)/shard_map/all_gather | solution.py:62
  8.6 225.9 %all-gather.6.cloned.1.call-start = ((), (), s32[]{:S(2)}) async-start(), calls=%async_computation.4 | async-start | bytes 2228224 | tf_op jit(solution)/shard_map/all_gather | solution.py:90
  101.8 4.2 %copy-start.4 = (s32[1,2,2,2]{3,2,1,0:T(2,128)S(1)}, s32[1,2,2,2]{3,2,1,0:T(2,128)}, u32[]{:S(2)}) copy-start(s32[1,2,2,2]{3,2,1,0:T(2,128)} %param.9) | copy-start | bytes 100
  105.3 0.7 copy-start.1
  239.7 21.7 %all-to-all-start.2 = ((bf16[16,64,256]{2,1,0:T(8,128)(2,1)}), bf16[16,64,256]{2,1,0:T(8,128)(2,1)S(1)}, u32[]{:S(2)}, u32[]{:S(2)}) async-start(bf16[16,64,256]{2,1,0:T(8,128)(2,1)} %bitcast.28), calls=%async_computation.2 | async-start | bytes 1048576 | tf_op jit(solution)/shard_map/all_to_all | solution.py:47
  261.5 60.0 %all-to-all-start.1 = ((bf16[32,256,128]{1,2,0:T(8,128)(2,1)}), bf16[32,256,128]{1,2,0:T(8,128)(2,1)S(1)}, u32[]{:S(2)}, u32[]{:S(2)}) async-start(bf16[32,256,128]{1,2,0:T(8,128)(2,1)} %bitcast.105), calls=%async_computation.1 | async-start | bytes 4194304 | tf_op jit(solution)/shard_map/all_to_all | solution.py:40
  321.4 53.6 %all-to-all-start = ((bf16[32,256,128]{1,2,0:T(8,128)(2,1)}), bf16[32,256,128]{1,2,0:T(8,128)(2,1)}, u32[]{:S(2)}, u32[]{:S(2)}) async-start(bf16[32,256,128]{1,2,0:T(8,128)(2,1)} %bitcast.106), calls=%async_computation | async-start | bytes 4194304 | tf_op jit(solution)/shard_map/all_to_all | solution.py:40
  375.9 23.4 %all-to-all-start.3 = ((bf16[16,64,256]{2,1,0:T(8,128)(2,1)}), bf16[16,64,256]{2,1,0:T(8,128)(2,1)S(1)}, u32[]{:S(2)}, u32[]{:S(2)}) async-start(bf16[16,64,256]{2,1,0:T(8,128)(2,1)} %broadcast_in_dim.11), calls=%async_computation.3 | async-start | bytes 1048576 | tf_op jit(solution)/shard_map/all_to_all | solution.py:50
  381.9 2.2 copy-start.2
  381.9 2.2 copy-start.3
  384.1 16.0 %collective-permute-start = (bf16[1,128,256]{2,1,0:T(8,128)(2,1)S(1)}, bf16[1,128,256]{2,1,0:T(8,128)(2,1)S(1)}, u32[]{:S(2)}, u32[]{:S(2)}) collective-permute-start(bf16[1,128,256]{2,1,0:T(8,128)(2,1)S(1)} %get-tuple-element.53), channel_id=1, source_target_pairs={{0,32},{32,64},{64,96},{96,128},{128,160},{160,192},{192,224},{224... | collective-permute-start | bytes 196616 | tf_op jit(solution)/shard_map/ppermute | solution.py:14
  385.8 14.4 %collective-permute-start.1 = (bf16[1,128,256]{2,1,0:T(8,128)(2,1)S(1)}, bf16[1,128,256]{2,1,0:T(8,128)(2,1)S(1)}, u32[]{:S(2)}, u32[]{:S(2)}) collective-permute-start(bf16[1,128,256]{2,1,0:T(8,128)(2,1)S(1)} %get-tuple-element.52), channel_id=1, source_target_pairs={{0,480},{32,0},{64,32},{96,64},{128,96},{160,128},{192,160},{224,1... | collective-permute-start | bytes 196616 | tf_op jit(solution)/shard_map/ppermute | solution.py:14
Sparse Core Ops, SparseCore 0:
  11.0 90.6 all-gather.7
  104.8 80.8 all-gather.9
  188.4 46.0 all-gather.5
where the time goes:
time: 409 us; the launch traced here: 408 us
  waiting for transfers between devices  336 us (82%)
  starting transfers between devices  26.6 us (7%)
  local copies, waits for them, and re-layouts  14.6 us (4%)
  between operations  14 us (3%)
  matrix products  13.5 us (3%)
    all_to_all x2, waiting for transfers between devices, head_sum(): moved = lax.all_to_all(parts, axis, 0, 0, tiled=True)  93.8 us
    all_gather x1, waiting for transfers between devices, per_device(): lax.all_gather(local_rows, 'mp', axis=2, tiled=True)  89.2 us
    all_gather x1, waiting for transfers between devices, per_device(): lax.all_gather(local_carry, 'mp', axis=1, tiled=True)  79.5 us
    all_gather x1, waiting for transfers between devices, per_device(): collected = lax.all_gather(encoded, 'segment', axis=0, tiled=True)  45.9 us
    all_to_all x2, starting transfers between devices, head_sum(): moved = lax.all_to_all(parts, axis, 0, 0, tiled=True)  14.4 us
    all_to_all x1, waiting for transfers between devices, segment_sum(): return lax.all_to_all(spread, axis, 0, 0, tiled=True).reshape(contrib.shape)  13.4 us
    all_to_all x1, waiting for transfers between devices, segment_sum(): moved = lax.all_to_all(parts, axis, 0, 0, tiled=True)  13.1 us
  transfers between devices with their start and end apart: 9, of which 7 were waited for; matrix products, arithmetic and copies ran while one was open for 6% of the time, Pallas kernels for 0%

commit v1 on v0

--- a/solution.py
+++ b/solution.py
@@ -51,6 +51,16 @@
 
 
 def per_device(rows, carry, weights, neighbours):
+
+    def goods_scan(work_x):
+        along_axis = "segment"
+        n_shards = lax.axis_size(along_axis)
+        column = [n_shards if q == 0 else 1 for q in range(work_x.ndim)]
+        a_next = lax.all_to_all(
+            jnp.tile(work_x, column), split_axis=0, tiled=True, concat_axis=0, axis_name=along_axis
+        )
+        return a_next
+
     segments = lax.axis_size("segment")
     encoders = segments // 4
     first_encoder = segments - encoders
@@ -87,7 +97,7 @@
     encoded, queries = lax.cond(is_encoder, encode, decode)
     per_encoder = 2 * tokens // NBLEN
     pool_blocks = encoders * per_encoder
-    collected = lax.all_gather(encoded, "segment", axis=0, tiled=True)
+    collected = goods_scan(encoded)
     pool = collected[first_encoder * 2 * tokens :].reshape(pool_blocks, NBLEN, 2 * head)
     groups = tokens // GROUP
     local_nbr = neighbours[0]

time: 409 us -> 367 us (0.90)
  waiting for transfers between devices: 336 us -> 277 us
  starting transfers between devices: 26.6 us -> 44.1 us
    all_gather x1 -> x0, waiting for transfers between devices: 45.9 us -> none  [per_device(): collected = lax.all_gather(encoded, 'segment', axis=0, tiled=True)]
    all_gather x1, waiting for transfers between devices: 79.5 us -> 66 us  [per_device(): lax.all_gather(local_carry, 'mp', axis=1, tiled=True)]
    all_to_all x0 -> x1, starting transfers between devices: none -> 12.7 us  [goods_scan(): lax.all_to_all(jnp.tile(work_x, column), split_axis=0, tiled=True, concat...]
    all_to_all x1, starting transfers between devices: 4.42 us -> 10.9 us  [segment_sum(): moved = lax.all_to_all(parts, axis, 0, 0, tiled=True)]
  transfers between devices with their start and end apart: 9 -> 9, of which waited for: 7 -> 6; matrix products, arithmetic and copies ran while one was open for 6% -> 7% of each run, Pallas kernels for 0% -> 0%
where the time goes in v1:
time: 367 us; the launch traced here: 366 us
  waiting for transfers between devices  277 us (75%)
  starting transfers between devices  44.1 us (12%)
  local copies, waits for them, and re-layouts  14.5 us (4%)
  between operations  14.2 us (4%)
  matrix products  13.4 us (4%)
    all_to_all x2, waiting for transfers between devices, head_sum(): moved = lax.all_to_all(parts, axis, 0, 0, tiled=True)  93.8 us
    all_gather x1, waiting for transfers between devices, per_device(): lax.all_gather(local_rows, 'mp', axis=2, tiled=True)  89.3 us
    all_gather x1, waiting for transfers between devices, per_device(): lax.all_gather(local_carry, 'mp', axis=1, tiled=True)  66 us
    all_to_all x1, waiting for transfers between devices, segment_sum(): return lax.all_to_all(spread, axis, 0, 0, tiled=True).reshape(contrib.shape)  13.4 us
    all_to_all x1, waiting for transfers between devices, segment_sum(): moved = lax.all_to_all(parts, axis, 0, 0, tiled=True)  13.1 us
    all_to_all x2, starting transfers between devices, head_sum(): moved = lax.all_to_all(parts, axis, 0, 0, tiled=True)  12.7 us
    all_to_all x1, starting transfers between devices, goods_scan(): lax.all_to_all(jnp.tile(work_x, column), split_axis=0, tiled=True, concat...  12.7 us
    all_to_all x1, starting transfers between devices, segment_sum(): moved = lax.all_to_all(parts, axis, 0, 0, tiled=True)  10.9 us
  transfers between devices with their start and end apart: 9, of which 6 were waited for; matrix products, arithmetic and copies ran while one was open for 7% of the time, Pallas kernels for 0%

profile of v1, /device:TPU:1, one launch (start us, length us, event | category | flops | bytes accessed | tf_op | source)
XLA Modules:
  0.0 366.2 jit_solution(6764382085983045670)
XLA Ops:
  8.6 3.8 %slice_bitcast_fusion = (bf16[8192,128]{1,0:T(8,128)(2,1)}, bf16[8192,128]{1,0:T(8,128)(2,1)S(1)}) fusion(bf16[1,2,8192,128]{3,2,1,0:T(8,128)(2,1)} %param.8), kind=kLoop, calls=%fused_computation.16 | loop fusion | bytes 8388608 | tf_op jit(solution)/shard_map/squeeze | solution.py:78
  12.5 89.3 %all-gather.5.cloned.1.call-done = bf16[1,2,128,8192]{3,2,1,0:T(8,128)(2,1)} async-done(((bf16[1,2,128,256]{3,2,1,0:T(8,128)(2,1)}), bf16[1,2,128,8192]{3,2,1,0:T(8,128)(2,1)}) %all-gather.5.cloned.1.call-update) | async-done | bytes 4194320 | tf_op jit(solution)/shard_map/all_gather | solution.py:71
  101.8 3.5 conditional.1
  101.8 3.4 convolution_convert_fusion
  105.3 1.6 tile.2
  106.8 12.7 %all-to-all-start = ((bf16[16,256,256]{2,1,0:T(8,128)(2,1)}), bf16[16,256,256]{2,1,0:T(8,128)(2,1)S(1)}, u32[]{:S(2)}, u32[]{:S(2)}) async-start(bf16[16,256,256]{2,1,0:T(8,128)(2,1)} %tile.2), calls=%async_computation | async-start | bytes 4194304 | tf_op jit(solution)/shard_map/all_to_all | solution.py:59
  119.8 66.0 %all-gather.7.cloned.1.call-done = bf16[1,128,8192]{2,1,0:T(8,128)(2,1)} async-done(((bf16[1,128,256]{2,1,0:T(8,128)(2,1)}), bf16[1,128,8192]{2,1,0:T(8,128)(2,1)}) %all-gather.7.cloned.1.call-update) | async-done | bytes 2097168 | tf_op jit(solution)/shard_map/all_gather | solution.py:72
  185.8 2.9 fusion.11
  192.0 0.9 copy.19
  192.9 10.9 %all-to-all-start.3 = ((bf16[16,64,256]{2,1,0:T(8,128)(2,1)}), bf16[16,64,256]{2,1,0:T(8,128)(2,1)S(1)}, u32[]{:S(2)}, u32[]{:S(2)}) async-start(bf16[16,64,256]{2,1,0:T(8,128)(2,1)} %bitcast.28), calls=%async_computation.3 | async-start | bytes 1048576 | tf_op jit(solution)/shard_map/all_to_all | solution.py:47
  204.1 2.3 convolution_convert_fusion.3
  206.4 1.6 copy.25
  208.0 13.1 %all-to-all-done.3 = bf16[16,64,256]{2,1,0:T(8,128)(2,1)S(1)} async-done(((bf16[16,64,256]{2,1,0:T(8,128)(2,1)}), bf16[16,64,256]{2,1,0:T(8,128)(2,1)S(1)}, u32[]{:S(2)}, u32[]{:S(2)}) %all-to-all-start.3) | async-done | bytes 524320 | tf_op jit(solution)/shard_map/all_to_all | solution.py:47
  221.1 7.6 %all-to-all-start.2 = ((bf16[32,256,128]{1,2,0:T(8,128)(2,1)}), bf16[32,256,128]{1,2,0:T(8,128)(2,1)S(1)}, u32[]{:S(2)}, u32[]{:S(2)}) async-start(bf16[32,256,128]{1,2,0:T(8,128)(2,1)} %bitcast.105), calls=%async_computation.2 | async-start | bytes 4194304 | tf_op jit(solution)/shard_map/all_to_all | solution.py:40
  230.0 2.3 convolution_convert_fusion.4
  232.3 1.6 copy.26
  234.0 45.4 %all-to-all-done.2 = bf16[32,256,128]{1,2,0:T(8,128)(2,1)S(1)} async-done(((bf16[32,256,128]{1,2,0:T(8,128)(2,1)}), bf16[32,256,128]{1,2,0:T(8,128)(2,1)S(1)}, u32[]{:S(2)}, u32[]{:S(2)}) %all-to-all-start.2) | async-done | bytes 2097184 | tf_op jit(solution)/shard_map/all_to_all | solution.py:40
  279.4 5.1 %all-to-all-start.1 = ((bf16[32,256,128]{1,2,0:T(8,128)(2,1)}), bf16[32,256,128]{1,2,0:T(8,128)(2,1)}, u32[]{:S(2)}, u32[]{:S(2)}) async-start(bf16[32,256,128]{1,2,0:T(8,128)(2,1)} %bitcast.106), calls=%async_computation.1 | async-start | bytes 4194304 | tf_op jit(solution)/shard_map/all_to_all | solution.py:40
  284.6 48.3 %all-to-all-done.1 = bf16[32,256,128]{1,2,0:T(8,128)(2,1)} async-done(((bf16[32,256,128]{1,2,0:T(8,128)(2,1)}), bf16[32,256,128]{1,2,0:T(8,128)(2,1)}, u32[]{:S(2)}, u32[]{:S(2)}) %all-to-all-start.1) | async-done | bytes 2097184 | tf_op jit(solution)/shard_map/all_to_all | solution.py:40
  333.8 6.0 %all-to-all-start.4 = ((bf16[16,64,256]{2,1,0:T(8,128)(2,1)}), bf16[16,64,256]{2,1,0:T(8,128)(2,1)S(1)}, u32[]{:S(2)}, u32[]{:S(2)}) async-start(bf16[16,64,256]{2,1,0:T(8,128)(2,1)} %broadcast_in_dim.11), calls=%async_computation.4 | async-start | bytes 1048576 | tf_op jit(solution)/shard_map/all_to_all | solution.py:50
  340.2 1.9 convert_reduce_fusion.1
  342.1 1.7 collective-permute-start
  343.8 13.4 %all-to-all-done.4 = bf16[16,64,256]{2,1,0:T(8,128)(2,1)S(1)} async-done(((bf16[16,64,256]{2,1,0:T(8,128)(2,1)}), bf16[16,64,256]{2,1,0:T(8,128)(2,1)S(1)}, u32[]{:S(2)}, u32[]{:S(2)}) %all-to-all-start.4) | async-done | bytes 524320 | tf_op jit(solution)/shard_map/all_to_all | solution.py:50
  357.2 0.9 reshape_reshape.7
  (45 shorter events, 9.0 us)
Async XLA Ops:
  7.2 94.6 %all-gather.5.cloned.1.call-start = ((), (), s32[]{:S(2)}) async-start(), calls=%async_computation.5 | async-start | bytes 4325376 | tf_op jit(solution)/shard_map/all_gather | solution.py:71
  7.9 177.9 %all-gather.7.cloned.1.call-start = ((), (), s32[]{:S(2)}) async-start(), calls=%async_computation.6 | async-start | bytes 2162688 | tf_op jit(solution)/shard_map/all_gather | solution.py:72
  106.8 12.7 %copy-start.3 = (s32[1,2,2,2]{3,2,1,0:T(2,128)S(1)}, s32[1,2,2,2]{3,2,1,0:T(2,128)}, u32[]{:S(2)}) copy-start(s32[1,2,2,2]{3,2,1,0:T(2,128)} %param.9) | copy-start | bytes 100
  106.8 81.9 %all-to-all-start = ((bf16[16,256,256]{2,1,0:T(8,128)(2,1)}), bf16[16,256,256]{2,1,0:T(8,128)(2,1)S(1)}, u32[]{:S(2)}, u32[]{:S(2)}) async-start(bf16[16,256,256]{2,1,0:T(8,128)(2,1)} %tile.2), calls=%async_computation | async-start | bytes 4194304 | tf_op jit(solution)/shard_map/all_to_all | solution.py:59
  192.9 28.2 %all-to-all-start.3 = ((bf16[16,64,256]{2,1,0:T(8,128)(2,1)}), bf16[16,64,256]{2,1,0:T(8,128)(2,1)S(1)}, u32[]{:S(2)}, u32[]{:S(2)}) async-start(bf16[16,64,256]{2,1,0:T(8,128)(2,1)} %bitcast.28), calls=%async_computation.3 | async-start | bytes 1048576 | tf_op jit(solution)/shard_map/all_to_all | solution.py:47
  221.1 58.3 %all-to-all-start.2 = ((bf16[32,256,128]{1,2,0:T(8,128)(2,1)}), bf16[32,256,128]{1,2,0:T(8,128)(2,1)S(1)}, u32[]{:S(2)}, u32[]{:S(2)}) async-start(bf16[32,256,128]{1,2,0:T(8,128)(2,1)} %bitcast.105), calls=%async_computation.2 | async-start | bytes 4194304 | tf_op jit(solution)/shard_map/all_to_all | solution.py:40
  279.4 53.6 %all-to-all-start.1 = ((bf16[32,256,128]{1,2,0:T(8,128)(2,1)}), bf16[32,256,128]{1,2,0:T(8,128)(2,1)}, u32[]{:S(2)}, u32[]{:S(2)}) async-start(bf16[32,256,128]{1,2,0:T(8,128)(2,1)} %bitcast.106), calls=%async_computation.1 | async-start | bytes 4194304 | tf_op jit(solution)/shard_map/all_to_all | solution.py:40
  333.8 23.4 %all-to-all-start.4 = ((bf16[16,64,256]{2,1,0:T(8,128)(2,1)}), bf16[16,64,256]{2,1,0:T(8,128)(2,1)S(1)}, u32[]{:S(2)}, u32[]{:S(2)}) async-start(bf16[16,64,256]{2,1,0:T(8,128)(2,1)} %broadcast_in_dim.11), calls=%async_computation.4 | async-start | bytes 1048576 | tf_op jit(solution)/shard_map/all_to_all | solution.py:50
  339.8 2.2 copy-start.1
  339.8 2.2 copy-start.2
  342.1 16.0 %collective-permute-start = (bf16[1,128,256]{2,1,0:T(8,128)(2,1)S(1)}, bf16[1,128,256]{2,1,0:T(8,128)(2,1)S(1)}, u32[]{:S(2)}, u32[]{:S(2)}) collective-permute-start(bf16[1,128,256]{2,1,0:T(8,128)(2,1)S(1)} %get-tuple-element.53), channel_id=1, source_target_pairs={{0,32},{32,64},{64,96},{96,128},{128,160},{160,192},{192,224},{224... | collective-permute-start | bytes 196616 | tf_op jit(solution)/shard_map/ppermute | solution.py:14
  343.7 14.4 %collective-permute-start.1 = (bf16[1,128,256]{2,1,0:T(8,128)(2,1)S(1)}, bf16[1,128,256]{2,1,0:T(8,128)(2,1)S(1)}, u32[]{:S(2)}, u32[]{:S(2)}) collective-permute-start(bf16[1,128,256]{2,1,0:T(8,128)(2,1)S(1)} %get-tuple-element.52), channel_id=1, source_target_pairs={{0,480},{32,0},{64,32},{96,64},{128,96},{160,128},{192,160},{224,1... | collective-permute-start | bytes 196616 | tf_op jit(solution)/shard_map/ppermute | solution.py:14
Sparse Core Ops, SparseCore 0:
  11.0 90.6 all-gather.4
  104.8 80.8 all-gather.6
